TPU v7x, 32 devices: a whole 2x2x4 slice. The times are simulated.
32 devices in a mesh: groups: 2 (over y), space: 8 (over z, core), member: 2 (over x).
Axes of the slice: x: 2, y: 2, z: 4, core: 2. Of those that a mesh axis runs over, the one named last changes fastest.
Arguments:
- features: bfloat16 [4, 256, 128, 256], P(('groups', 'member'), None, 'space'), parts along dimension 0, may hold values from -6 to 6
- views: int32 [4], P('groups'), parts along dimension 0, may hold values from 8 to 29
- conv_first: bfloat16 [3, 3, 256, 256], replicated, may hold values from -0.125 to 0.125
- bias_first: float32 [256], replicated, may hold values from -3 to 3
- conv_second: bfloat16 [3, 3, 256, 256], replicated, may hold values from -0.125 to 0.125
- bias_second: float32 [256], replicated, may hold values from -3 to 3
- classify: bfloat16 [19, 256], replicated, may hold values from -0.375 to 0.375
- class_bias: float32 [19], replicated, may hold values from -3 to 3
Outputs:
- ensemble_logits: float32 [1024, 19, 1024], P(('groups', 'space', 'member')), parts along dimension 0
There are 2 independent parts, one for each index of `groups`. A program takes and returns all parts, laid end to end along the dimension named above; an argument that names none is the same for every part. Nothing has to cross between parts.
All inputs are finite; a program needn't handle non-finite values.
Results may differ from a plain program's by a relative error of at most 0.0035.
Values may be sent and summed in bfloat16 or wider, within the bound.
No kernel may reach another device: no remote copies, remote signals or barrier semaphores. Data moves between devices by JAX's collectives and lax.ppermute only.
A program may use at most 128 MiB of HBM per device.

v0:
```python
import jax
import jax.numpy as jnp
from jax import lax
from jax.sharding import PartitionSpec as P

UP = 4


def with_halo(block, sides, width):
    for axis, dim in sides:
        count = lax.axis_size(axis)
        forward = [(i, i + 1) for i in range(count - 1)]
        backward = [(target, source) for source, target in forward]
        low = lax.ppermute(
            lax.slice_in_dim(block, block.shape[dim] - width, None, axis=dim), axis, forward
        )
        high = lax.ppermute(lax.slice_in_dim(block, 0, width, axis=dim), axis, backward)
        block = jnp.concatenate([low, block, high], axis=dim)
    return block


def resize_matrix(positions, out_len, valid, in_len):
    numer = (2 * positions + 1) * valid - out_len
    denom = 2 * out_len
    lower = numer // denom
    frac = (numer - lower * denom).astype(jnp.float32) / denom
    below = numer < 0
    frac = jnp.where(below, jnp.float32(0.0), frac)
    lower = jnp.where(below, 0, lower)
    top_index = valid - 1
    over = lower >= top_index
    frac = jnp.where(over, jnp.float32(0.0), frac)
    lower = jnp.where(over, top_index, lower)
    columns = jnp.arange(in_len, dtype=jnp.int32)
    first = jnp.where(columns[None, :] == lower[:, None], 1.0 - frac[:, None], jnp.float32(0.0))
    second = jnp.where(columns[None, :] == lower[:, None] + 1, frac[:, None], jnp.float32(0.0))
    return (first + second).astype(jnp.bfloat16)


def convolve(field, weights):
    height, width = (field.shape[1], field.shape[2])
    padded = with_halo(field, (("space", 1),), 1)
    padded = jnp.pad(padded, ((0, 0), (0, 0), (1, 1)))
    total = jnp.zeros((weights.shape[2], height, width), jnp.float32)
    for row_tap in range(3):
        for col_tap in range(3):
            window = padded[:, row_tap : row_tap + height, col_tap : col_tap + width]
            total = total + jnp.einsum(
                "oc,cyx->oyx", weights[row_tap, col_tap], window, preferred_element_type=jnp.float32
            )
    return total


def window_start(numer, first_row, full_rows, out_rows, window_rows):
    valid = full_rows * numer // 14
    numer_pos = (2 * first_row + 1) * valid - out_rows
    lower = numer_pos // (2 * out_rows)
    lower = jnp.where(numer_pos < 0, 0, lower)
    lower = jnp.where(lower >= valid - 1, valid - 1, lower)
    return jnp.clip(lower, 0, full_rows - window_rows)


def column_table(numer, flip, cols, out_cols):
    valid_cols = cols * numer // 14
    col_pos = jnp.arange(out_cols, dtype=jnp.int32)
    col_pos = jnp.where(flip == 1, out_cols - 1 - col_pos, col_pos)
    return resize_matrix(col_pos, out_cols, valid_cols, cols)


def shards(features, views, conv_first, bias_first, conv_second, bias_second, classify, class_bias):
    feat = features[0]
    rows_dev, cols = (feat.shape[1], feat.shape[2])
    spaces = lax.axis_size("space")
    full_rows = rows_dev * spaces
    place = lax.axis_index("space")
    member_index = lax.axis_index("member")
    members = views.shape[0]
    picked = jnp.arange(members, dtype=jnp.int32) == member_index
    code = jnp.sum(jnp.where(picked, views, 0))
    numer = code // 2
    valid_rows = full_rows * numer // 14
    valid_cols = cols * numer // 14
    row_ids = place * rows_dev + jnp.arange(rows_dev, dtype=jnp.int32)
    row_ok = row_ids < valid_rows
    col_ok = jnp.arange(cols, dtype=jnp.int32) < valid_cols
    mask = (row_ok[:, None] & col_ok[None, :]).astype(jnp.float32)
    first = feat * mask.astype(jnp.bfloat16)
    hidden = (jax.nn.relu(convolve(first, conv_first) + bias_first[:, None, None]) * mask).astype(
        jnp.bfloat16
    )
    second = (
        jax.nn.relu(convolve(hidden, conv_second) + bias_second[:, None, None]) * mask
    ).astype(jnp.bfloat16)
    logits = (
        jnp.einsum("kc,cyx->kyx", classify, second, preferred_element_type=jnp.float32)
        + class_bias[:, None, None]
    ).astype(jnp.bfloat16)
    out_rows = UP * full_rows
    out_cols = UP * cols
    own_rows = out_rows // spaces
    part_rows = own_rows // members
    window_rows = (part_rows - 1) // UP + 3
    gathered = lax.all_gather(logits, "space", axis=1, tiled=True)
    pieces = []
    for target in range(members):
        first_row = place * own_rows + target * part_rows
        begin = window_start(numer, first_row, full_rows, out_rows, window_rows)
        pieces.append(lax.dynamic_slice_in_dim(gathered, begin, window_rows, 1))
    outgoing = jnp.stack(pieces, 0)
    incoming = lax.all_to_all(outgoing, "member", split_axis=0, concat_axis=0, tiled=True)
    own_first = place * own_rows + member_index * part_rows
    positions = own_first + jnp.arange(part_rows, dtype=jnp.int32)
    result = jnp.zeros((part_rows, logits.shape[0], out_cols), jnp.float32)
    for source in range(members):
        source_numer = views[source] // 2
        source_flip = views[source] % 2
        source_valid = full_rows * source_numer // 14
        begin = window_start(source_numer, own_first, full_rows, out_rows, window_rows)
        source_cols = column_table(source_numer, source_flip, cols, out_cols)
        row_table = resize_matrix(positions, out_rows, source_valid, full_rows)
        row_part = lax.dynamic_slice_in_dim(row_table, begin, window_rows, 1)
        widened = jnp.einsum(
            "cyx,jx->cyj", incoming[source], source_cols, preferred_element_type=jnp.float32
        ).astype(jnp.bfloat16)
        result = result + jnp.einsum(
            "iy,cyj->icj", row_part, widened, preferred_element_type=jnp.float32
        )
    return result


def solution(mesh):
    placed = (
        P(("groups", "member"), None, "space", None),
        P("groups"),
        P(),
        P(),
        P(),
        P(),
        P(),
        P(),
    )
    return jax.shard_map(
        shards,
        mesh=mesh,
        in_specs=placed,
        out_specs=P(("groups", "space", "member"), None, None),
        check_vma=False,
    )
```

profile of v0, /device:TPU:0, one launch (start us, length us, event | category | flops | bytes accessed | tf_op | source)
XLA Modules:
  0.0 144.4 jit_solution(15678336219757409563)
XLA Ops:
  6.5 0.0 all-gather.2.cloned.1.call-start
  6.5 1.3 fusion.170
  10.5 4.3 %copy.22 = bf16[1,256,16,256]{1,3,2,0:T(8,128)(2,1)} copy(bf16[1,256,16,256]{3,2,1,0:T(8,128)(2,1)} %param.8) | data formatting | bytes 4194304 | tf_op args[0]
  14.8 0.1 fusion.147
  14.9 2.1 %bitcast_multiply_fusion = bf16[256,16,256]{0,2,1:T(8,128)(2,1)S(1)} fusion(bf16[1,256,16,256]{1,3,2,0:T(8,128)(2,1)} %copy.22, bf16[16,256]{1,0:T(8,128)(2,1)S(1)} %get-tuple-element.21), kind=kLoop, calls=%fused_computation.54 | loop fusion | flops 1048576 | bytes 4202496 | tf_op jit(solution)/shard_map/mul | solution.py:87
  16.9 0.0 copy-start.2
  17.0 2.5 %collective-permute-start = (bf16[256,1,256]{0,2,1:T(8,128)(2,1)S(1)}, bf16[256,1,256]{0,2,1:T(8,128)(2,1)S(1)}, u32[]{:S(2)}, u32[]{:S(2)}) collective-permute-start(bf16[256,1,256]{0,2,1:T(8,128)(2,1)S(1)} %get-tuple-element.15), channel_id=1, source_target_pairs={{0,2},{2,4},{4,6},{6,8},{8,10},{10,12},{12,14},{1,3},{3,5},{5,7},{... | collective-permute-start | bytes 393224 | tf_op jit(solution)/shard_map/ppermute | solution.py:14
  19.5 1.3 collective-permute-start.1
  20.8 0.1 multiply_bitcast_fusion
  20.9 0.0 copy-done.2
  20.9 1.7 %fusion.52 = f32[16,256,256]{2,1,0:T(8,128)S(1)} fusion(bf16[256,16,256]{2,1,0:T(8,128)(2,1)S(1)} %multiply_bitcast_fusion, bf16[3,3,256,256]{3,2,1,0:T(8,128)(2,1)S(1)} %copy-done.2), kind=kOutput, calls=%fused_computation.55 | convolution fusion | flops 536870912 | bytes 6422528 | tf_op jit(solution)/shard_map/oc,cyx->oyx/dot_general | solution.py:48
  22.6 0.0 collective-permute-done
  22.6 2.3 %collective-permute-done.1 = bf16[256,1,256]{0,2,1:T(8,128)(2,1)S(1)} collective-permute-done((bf16[256,1,256]{0,2,1:T(8,128)(2,1)S(1)}, bf16[256,1,256]{0,2,1:T(8,128)(2,1)S(1)}, u32[]{:S(2)}, u32[]{:S(2)}) %collective-permute-start.1) | collective-permute-done | bytes 131104 | tf_op jit(solution)/shard_map/ppermute | solution.py:17
  24.9 0.8 fusion.5
  25.8 0.7 fusion.40
  26.5 2.8 %fusion.42 = f32[16,256,256]{2,1,0:T(8,128)} fusion(bf16[256,18,258]{0,2,1:T(8,128)(2,1)S(1)} %fusion.5, bf16[3,3,256,256]{3,2,1,0:T(8,128)(2,1)S(1)} %copy-done.2), kind=kOutput, calls=%fused_computation.44 | convolution fusion | flops 536870912 | bytes 6422528 | tf_op jit(solution)/shard_map/oc,cyx->oyx/dot_general | solution.py:48
  29.3 2.7 %fusion.44 = f32[16,256,256]{2,1,0:T(8,128)} fusion(bf16[256,18,258]{0,2,1:T(8,128)(2,1)S(1)} %fusion.5, bf16[3,3,256,256]{3,2,1,0:T(8,128)(2,1)S(1)} %copy-done.2), kind=kOutput, calls=%fused_computation.46 | convolution fusion | flops 536870912 | bytes 6422528 | tf_op jit(solution)/shard_map/oc,cyx->oyx/dot_general | solution.py:48
  32.0 2.7 %fusion.46 = f32[16,256,256]{2,1,0:T(8,128)} fusion(bf16[256,18,258]{0,2,1:T(8,128)(2,1)S(1)} %fusion.5, bf16[3,3,256,256]{3,2,1,0:T(8,128)(2,1)S(1)} %copy-done.2), kind=kOutput, calls=%fused_computation.48 | convolution fusion | flops 536870912 | bytes 6422528 | tf_op jit(solution)/shard_map/oc,cyx->oyx/dot_general | solution.py:48
  34.7 2.7 %fusion.48 = f32[16,256,256]{2,1,0:T(8,128)} fusion(bf16[256,18,258]{0,2,1:T(8,128)(2,1)S(1)} %fusion.5, bf16[3,3,256,256]{3,2,1,0:T(8,128)(2,1)S(1)} %copy-done.2), kind=kOutput, calls=%fused_computation.50 | convolution fusion | flops 536870912 | bytes 6422528 | tf_op jit(solution)/shard_map/oc,cyx->oyx/dot_general | solution.py:48
  37.4 2.8 %fusion.6 = f32[16,256,256]{2,1,0:T(8,128)} fusion(bf16[256,16,256]{0,2,1:T(8,128)(2,1)S(1)} %bitcast_multiply_fusion, bf16[256,1,256]{0,2,1:T(8,128)(2,1)S(1)} %collective-permute-done, bf16[3,3,256,256]{3,2,1,0:T(8,128)(2,1)S(1)} %copy-done.2), kind=kOutput, calls=%fused_computation.12 | convolution fusion | flops 541327360 | bytes 6553600 | tf_op jit(solution)/shard_map/oc,cyx->oyx/dot_general | solution.py:48
  40.2 2.7 %fusion.10 = f32[16,256,256]{2,1,0:T(8,128)} fusion(bf16[256,1,256]{0,2,1:T(8,128)(2,1)S(1)} %collective-permute-done.1, bf16[256,16,256]{0,2,1:T(8,128)(2,1)S(1)} %bitcast_multiply_fusion, bf16[3,3,256,256]{3,2,1,0:T(8,128)(2,1)S(1)} %copy-done.2), kind=kOutput, calls=%fused_computation.16 | convolution fusion | flops 541327360 | bytes 6553600 | tf_op jit(solution)/shard_map/oc,cyx->oyx/dot_general | solution.py:48
  42.8 9.7 %fusion.54 = bf16[256,16,256]{0,2,1:T(8,128)(2,1)S(1)} fusion(f32[16,256]{1,0:T(8,128)S(1)} %get-tuple-element.22, f32[256]{0:T(256)S(1)} %copy-done.5, bf16[256,18,258]{0,2,1:T(8,128)(2,1)S(1)} %fusion.5, f32[16,256,256]{2,1,0:T(8,128)} %fusion.10, f32[16,256,256]{2,1,0:T(8,128)S(1)} %fusion.40, f32[16,256,256]{2,1,0:T(8,128)} %fusion.42, ...), kind=kOutput, calls=%fused_computation.59 | convolution fusion | flops 549453824 | bytes 37897216 | tf_op jit(solution)/shard_map/oc,cyx->oyx/dot_general | solution.py:48
  52.6 5.4 %collective-permute-start.2 = (bf16[256,1,256]{0,2,1:T(8,128)(2,1)S(1)}, bf16[256,1,256]{0,2,1:T(8,128)(2,1)S(1)}, u32[]{:S(2)}, u32[]{:S(2)}) collective-permute-start(bf16[256,1,256]{0,2,1:T(8,128)(2,1)S(1)} %get-tuple-element.13), channel_id=1, source_target_pairs={{0,2},{2,4},{4,6},{6,8},{8,10},{10,12},{12,14},{1,3},{3,5},{5,7},{... | collective-permute-start | bytes 393224 | tf_op jit(solution)/shard_map/ppermute | solution.py:14
  58.1 1.5 %collective-permute-start.3 = (bf16[256,1,256]{0,2,1:T(8,128)(2,1)S(1)}, bf16[256,1,256]{0,2,1:T(8,128)(2,1)S(1)}, u32[]{:S(2)}, u32[]{:S(2)}) collective-permute-start(bf16[256,1,256]{0,2,1:T(8,128)(2,1)S(1)} %get-tuple-element.14), channel_id=1, source_target_pairs={{2,0},{4,2},{6,4},{8,6},{10,8},{12,10},{14,12},{3,1},{5,3},{7,5},{... | collective-permute-start | bytes 393224 | tf_op jit(solution)/shard_map/ppermute | solution.py:17
  59.5 3.6 %fusion.108 = f32[16,256,256]{2,1,0:T(8,128)} fusion(bf16[256,16,256]{0,2,1:T(8,128)(2,1)S(1)} %fusion.54, bf16[3,3,256,256]{3,2,1,0:T(8,128)(2,1)} %param.12), kind=kOutput, calls=%fused_computation.91 | convolution fusion | flops 536870912 | bytes 6422528 | tf_op jit(solution)/shard_map/oc,cyx->oyx/dot_general | solution.py:48
  63.1 0.0 collective-permute-done.2
  63.1 0.0 collective-permute-done.3
  63.1 0.9 select_maximum_fusion
  64.0 0.4 copy-done.3
  64.4 2.8 %fusion.26 = f32[16,256,256]{2,1,0:T(8,128)} fusion(bf16[256,18,258]{0,2,1:T(8,128)(2,1)S(1)} %select_maximum_fusion, bf16[3,3,256,256]{3,2,1,0:T(8,128)(2,1)S(1)} %copy-done.3), kind=kOutput, calls=%fused_computation.30 | convolution fusion | flops 536870912 | bytes 6422528 | tf_op jit(solution)/shard_map/oc,cyx->oyx/dot_general | solution.py:48
  67.2 2.7 %fusion.28 = f32[16,256,256]{2,1,0:T(8,128)} fusion(bf16[256,18,258]{0,2,1:T(8,128)(2,1)S(1)} %select_maximum_fusion, bf16[3,3,256,256]{3,2,1,0:T(8,128)(2,1)S(1)} %copy-done.3), kind=kOutput, calls=%fused_computation.32 | convolution fusion | flops 536870912 | bytes 6422528 | tf_op jit(solution)/shard_map/oc,cyx->oyx/dot_general | solution.py:48
  69.9 2.7 %fusion.30 = f32[16,256,256]{2,1,0:T(8,128)} fusion(bf16[256,18,258]{0,2,1:T(8,128)(2,1)S(1)} %select_maximum_fusion, bf16[3,3,256,256]{3,2,1,0:T(8,128)(2,1)S(1)} %copy-done.3), kind=kOutput, calls=%fused_computation.34 | convolution fusion | flops 536870912 | bytes 6422528 | tf_op jit(solution)/shard_map/oc,cyx->oyx/dot_general | solution.py:48
  72.6 2.8 %fusion.32 = f32[16,256,256]{2,1,0:T(8,128)} fusion(bf16[256,18,258]{0,2,1:T(8,128)(2,1)S(1)} %select_maximum_fusion, bf16[3,3,256,256]{3,2,1,0:T(8,128)(2,1)S(1)} %copy-done.3), kind=kOutput, calls=%fused_computation.36 | convolution fusion | flops 536870912 | bytes 6422528 | tf_op jit(solution)/shard_map/oc,cyx->oyx/dot_general | solution.py:48
  75.4 2.7 %fusion.34 = f32[16,256,256]{2,1,0:T(8,128)} fusion(bf16[256,18,258]{0,2,1:T(8,128)(2,1)S(1)} %select_maximum_fusion, bf16[3,3,256,256]{3,2,1,0:T(8,128)(2,1)S(1)} %copy-done.3), kind=kOutput, calls=%fused_computation.38 | convolution fusion | flops 536870912 | bytes 6422528 | tf_op jit(solution)/shard_map/oc,cyx->oyx/dot_general | solution.py:48
  78.1 2.7 %fusion.14 = f32[16,256,256]{2,1,0:T(8,128)} fusion(bf16[256,16,256]{0,2,1:T(8,128)(2,1)S(1)} %fusion.54, bf16[256,1,256]{0,2,1:T(8,128)(2,1)S(1)} %collective-permute-done.2, bf16[3,3,256,256]{3,2,1,0:T(8,128)(2,1)S(1)} %copy-done.3), kind=kOutput, calls=%fused_computation.20 | convolution fusion | flops 541327360 | bytes 6553600 | tf_op jit(solution)/shard_map/oc,cyx->oyx/dot_general | solution.py:48
  80.8 2.7 %fusion.18 = f32[16,256,256]{2,1,0:T(8,128)} fusion(bf16[256,1,256]{0,2,1:T(8,128)(2,1)S(1)} %collective-permute-done.3, bf16[256,16,256]{0,2,1:T(8,128)(2,1)S(1)} %fusion.54, bf16[3,3,256,256]{3,2,1,0:T(8,128)(2,1)S(1)} %copy-done.3), kind=kOutput, calls=%fused_computation.24 | convolution fusion | flops 541327360 | bytes 6553600 | tf_op jit(solution)/shard_map/oc,cyx->oyx/dot_general | solution.py:48
  83.5 13.2 %fusion.72 = bf16[19,16,256]{2,0,1:T(8,128)(2,1)S(1)} fusion(f32[16,256]{1,0:T(8,128)S(1)} %get-tuple-element.22, f32[256]{0:T(256)S(1)} %copy-done.6, bf16[256,18,258]{0,2,1:T(8,128)(2,1)S(1)} %select_maximum_fusion, f32[16,256,256]{2,1,0:T(8,128)} %fusion.18, f32[16,256,256]{2,1,0:T(8,128)} %fusion.26, f32[16,256,256]{2,1,0:T(8,128)} %fusion.28, ...), kind=kOutput, calls=%fused_computation.65 | convolution fusion | flops 589455360 | bytes 35968512 | tf_op jit(solution)/shard_map/kc,cyx->kyx/dot_general | solution.py:95
  96.7 0.7 copy.25
  97.4 0.0 all-gather.2.cloned.1.call-update
  97.4 0.6 fusion.183
  103.7 18.8 %all-gather.2.cloned.1.call-done = bf16[19,128,256]{2,1,0:T(8,128)(2,1)} async-done(((bf16[19,16,256]{2,1,0:T(8,128)(2,1)}), bf16[19,128,256]{2,1,0:T(8,128)(2,1)}) %all-gather.2.cloned.1.call-update) | async-done | bytes 1245200 | tf_op jit(solution)/shard_map/all_gather | solution.py:103
  122.6 1.2 constant_dynamic-slice_fusion.1
  123.7 0.1 copy_bitcast_fusion.6
  123.8 0.7 pad_maximum_fusion
  124.5 3.4 %all-to-all-start = ((bf16[2,19,10,256]{3,1,2,0:T(8,128)(2,1)}), bf16[2,19,10,256]{3,1,2,0:T(8,128)(2,1)S(1)}, u32[]{:S(2)}, u32[]{:S(2)}) async-start(bf16[2,19,10,256]{3,1,2,0:T(8,128)(2,1)} %pad_maximum_fusion), calls=%async_computation | async-start | bytes 491520 | tf_op jit(solution)/shard_map/all_to_all | solution.py:110
  128.0 5.6 %all-to-all-done = bf16[2,19,10,256]{3,1,2,0:T(8,128)(2,1)S(1)} async-done(((bf16[2,19,10,256]{3,1,2,0:T(8,128)(2,1)}), bf16[2,19,10,256]{3,1,2,0:T(8,128)(2,1)S(1)}, u32[]{:S(2)}, u32[]{:S(2)}) %all-to-all-start) | async-done | bytes 194592 | tf_op jit(solution)/shard_map/all_to_all | solution.py:110
  133.6 1.2 fusion.61
  134.9 2.7 %convolution_add_fusion = f32[32,19,1024]{2,0,1:T(8,128)} fusion(f32[32,19,1024]{2,0,1:T(8,128)S(1)} %fusion.61, f32[1024]{0:T(1024)S(1)} %get-tuple-element.35, s32[1024]{0:T(1024)S(1)} %get-tuple-element.38, f32[1024]{0:T(1024)S(1)} %get-tuple-element.36, s32[1024]{0:T(1024)S(1)} %get-tuple-element.37, ...), kind=kOutput, calls=%fused_computation.58 | convolution fusion | flops 114458816 | bytes 5094916 | tf_op jit(solution)/shard_map/iy,cyj->icj/dot_general | solution.py:125
  (24 shorter events, 0.2 us)
Async XLA Ops:
  6.5 76.9 %copy-start = (bf16[19,256]{1,0:T(8,128)(2,1)S(1)}, bf16[19,256]{1,0:T(8,128)(2,1)}, u32[]{:S(2)}) copy-start(bf16[19,256]{1,0:T(8,128)(2,1)} %param.14) | copy-start | bytes 29188
  6.5 116.0 %all-gather.2.cloned.1.call-start = ((), (), s32[]{:S(2)}) async-start(), calls=%async_computation.1 | async-start | bytes 1400832 | tf_op jit(solution)/shard_map/all_gather | solution.py:103
  14.8 6.0 %copy-start.1 = (bf16[1,256,16,256]{3,2,1,0:T(8,128)(2,1)S(1)}, bf16[1,256,16,256]{3,2,1,0:T(8,128)(2,1)}, u32[]{:S(2)}) copy-start(bf16[1,256,16,256]{3,2,1,0:T(8,128)(2,1)} %param.8) | copy-start | bytes 6291460
  16.9 4.0 %copy-start.2 = (bf16[3,3,256,256]{3,2,1,0:T(8,128)(2,1)S(1)}, bf16[3,3,256,256]{3,2,1,0:T(8,128)(2,1)}, u32[]{:S(2)}) copy-start(bf16[3,3,256,256]{3,2,1,0:T(8,128)(2,1)} %param.10) | copy-start | bytes 3538948
  17.0 5.6 %collective-permute-start = (bf16[256,1,256]{0,2,1:T(8,128)(2,1)S(1)}, bf16[256,1,256]{0,2,1:T(8,128)(2,1)S(1)}, u32[]{:S(2)}, u32[]{:S(2)}) collective-permute-start(bf16[256,1,256]{0,2,1:T(8,128)(2,1)S(1)} %get-tuple-element.15), channel_id=1, source_target_pairs={{0,2},{2,4},{4,6},{6,8},{8,10},{10,12},{12,14},{1,3},{3,5},{5,7},{... | collective-permute-start | bytes 393224 | tf_op jit(solution)/shard_map/ppermute | solution.py:14
  19.5 5.4 %collective-permute-start.1 = (bf16[256,1,256]{0,2,1:T(8,128)(2,1)S(1)}, bf16[256,1,256]{0,2,1:T(8,128)(2,1)S(1)}, u32[]{:S(2)}, u32[]{:S(2)}) collective-permute-start(bf16[256,1,256]{0,2,1:T(8,128)(2,1)S(1)} %get-tuple-element.16), channel_id=1, source_target_pairs={{2,0},{4,2},{6,4},{8,6},{10,8},{12,10},{14,12},{3,1},{5,3},{7,5},{... | collective-permute-start | bytes 393224 | tf_op jit(solution)/shard_map/ppermute | solution.py:17
  40.2 2.7 %copy-start.5 = (f32[256]{0:T(256)S(1)}, f32[256]{0:T(256)}, u32[]{:S(2)}) copy-start(f32[256]{0:T(256)} %param.11) | copy-start | bytes 3076
  52.6 10.5 %collective-permute-start.2 = (bf16[256,1,256]{0,2,1:T(8,128)(2,1)S(1)}, bf16[256,1,256]{0,2,1:T(8,128)(2,1)S(1)}, u32[]{:S(2)}, u32[]{:S(2)}) collective-permute-start(bf16[256,1,256]{0,2,1:T(8,128)(2,1)S(1)} %get-tuple-element.13), channel_id=1, source_target_pairs={{0,2},{2,4},{4,6},{6,8},{8,10},{10,12},{12,14},{1,3},{3,5},{5,7},{... | collective-permute-start | bytes 393224 | tf_op jit(solution)/shard_map/ppermute | solution.py:14
  58.1 5.1 %collective-permute-start.3 = (bf16[256,1,256]{0,2,1:T(8,128)(2,1)S(1)}, bf16[256,1,256]{0,2,1:T(8,128)(2,1)S(1)}, u32[]{:S(2)}, u32[]{:S(2)}) collective-permute-start(bf16[256,1,256]{0,2,1:T(8,128)(2,1)S(1)} %get-tuple-element.14), channel_id=1, source_target_pairs={{2,0},{4,2},{6,4},{8,6},{10,8},{12,10},{14,12},{3,1},{5,3},{7,5},{... | collective-permute-start | bytes 393224 | tf_op jit(solution)/shard_map/ppermute | solution.py:17
  63.1 1.3 copy-start.3
  80.8 2.7 %copy-start.6 = (f32[256]{0:T(256)S(1)}, f32[256]{0:T(256)}, u32[]{:S(2)}) copy-start(f32[256]{0:T(256)} %param.13) | copy-start | bytes 3076
  80.8 2.7 %copy-start.7 = (f32[19]{0:T(128)S(1)}, f32[19]{0:T(128)}, u32[]{:S(2)}) copy-start(f32[19]{0:T(128)} %param.15) | copy-start | bytes 232
  83.5 13.9 %copy-start.4 = (s32[2]{0:T(128)S(1)}, s32[2]{0:T(128)}, u32[]{:S(2)}) copy-start(s32[2]{0:T(128)} %param.9) | copy-start | bytes 28
  124.5 9.1 %all-to-all-start = ((bf16[2,19,10,256]{3,1,2,0:T(8,128)(2,1)}), bf16[2,19,10,256]{3,1,2,0:T(8,128)(2,1)S(1)}, u32[]{:S(2)}, u32[]{:S(2)}) async-start(bf16[2,19,10,256]{3,1,2,0:T(8,128)(2,1)} %pad_maximum_fusion), calls=%async_computation | async-start | bytes 491520 | tf_op jit(solution)/shard_map/all_to_all | solution.py:110
Sparse Core Ops, SparseCore 0:
  97.5 24.9 all-gather.1
where the time goes:
time: 145 us; the launch traced here: 144 us
  matrix products  68.2 us (47%)
  waiting for transfers between devices  26.8 us (18%)
  between operations  21.8 us (15%)
  starting transfers between devices  14.2 us (10%)
  local copies, waits for them, and re-layouts  7.31 us (5%)
  other arithmetic  6.15 us (4%)
    dot_general x17, matrix products, convolve(): jnp.einsum('oc,cyx->oyx', weights[row_tap, col_tap], window, preferred_el...  51.1 us
    all_gather x1, waiting for transfers between devices, shards(): gathered = lax.all_gather(logits, 'space', axis=1, tiled=True)  18.8 us
    dot_general x1, matrix products, shards(): jnp.einsum('kc,cyx->kyx', classify, second, preferred_element_type=jnp.fl...  13.2 us
    ppermute x2, starting transfers between devices, with_halo(): lax.ppermute(lax.slice_in_dim(block, block.shape[dim] - width, None, axis...  7.95 us
    all_to_all x1, waiting for transfers between devices, shards(): lax.all_to_all(outgoing, 'member', split_axis=0, concat_axis=0, tiled=True)  5.63 us
    unnamed x17, local copies, waits for them, and re-layouts  4.69 us
    dot_general x2, matrix products, shards(): jnp.einsum('iy,cyj->icj', row_part, widened, preferred_element_type=jnp.f...  3.89 us
    all_to_all x1, starting transfers between devices, shards(): lax.all_to_all(outgoing, 'member', split_axis=0, concat_axis=0, tiled=True)  3.44 us
  transfers between devices with their start and end apart: 6, of which 3 were waited for; matrix products, arithmetic and copies ran while one was open for 4% of the time, Pallas kernels for 0%

commit v1 on v0

--- a/solution.py
+++ b/solution.py
@@ -4,6 +4,27 @@
 from jax.sharding import PartitionSpec as P
 
 UP = 4
+
+
+def joined_along(pieces, dim):
+    pieces = jnp.moveaxis(pieces, 0, dim)
+    lengths = pieces.shape
+    return pieces.reshape(*lengths[:dim], lengths[dim] * lengths[dim + 1], *lengths[dim + 2 :])
+
+
+def grow_blocks(array, axis):
+    size, mine = (lax.axis_size(axis), lax.axis_index(axis))
+    tiles, distance = (array[None], 1)
+    while distance < size:
+        other = lax.ppermute(tiles, axis, [(i, i ^ distance) for i in range(size)])
+        low = mine & distance == 0
+        tiles = jnp.concatenate([jnp.where(low, tiles, other), jnp.where(low, other, tiles)])
+        distance *= 2
+    return tiles
+
+
+def collect(x, axis, dim):
+    return joined_along(grow_blocks(x, axis), dim)
 
 
 def with_halo(block, sides, width):
@@ -100,7 +121,7 @@
     own_rows = out_rows // spaces
     part_rows = own_rows // members
     window_rows = (part_rows - 1) // UP + 3
-    gathered = lax.all_gather(logits, "space", axis=1, tiled=True)
+    gathered = collect(logits, "space", 1)
     pieces = []
     for target in range(members):
         first_row = place * own_rows + target * part_rows

time: 145 us -> 148 us (1.021)
  between operations: 21.8 us -> 8.3 us
  waiting for transfers between devices: 26.8 us -> 39.1 us
  starting transfers between devices: 14.2 us -> 19.7 us
  local copies, waits for them, and re-layouts: 7.31 us -> 5.49 us
    ppermute x0 -> x3, waiting for transfers between devices: none -> 31.8 us  [grow_blocks(): other = lax.ppermute(tiles, axis, [(i, i ^ distance) for i in range(size)])]
    all_gather x1 -> x0, waiting for transfers between devices: 18.8 us -> none  [shards(): gathered = lax.all_gather(logits, 'space', axis=1, tiled=True)]
    ppermute x0 -> x3, starting transfers between devices: none -> 5.57 us  [grow_blocks(): other = lax.ppermute(tiles, axis, [(i, i ^ distance) for i in range(size)])]
  transfers between devices with their start and end apart: 6 -> 8, of which waited for: 3 -> 5; matrix products, arithmetic and copies ran while one was open for 4% -> 4% of each run, Pallas kernels for 0% -> 0%
where the time goes in v1:
time: 148 us
  matrix products  68.3 us (46%)
  waiting for transfers between devices  39.1 us (26%)
  starting transfers between devices  19.7 us (13%)
  between operations  8.3 us (6%)
  other arithmetic  6.83 us (5%)
  local copies, waits for them, and re-layouts  5.49 us (4%)
    dot_general x17, matrix products, convolve(): jnp.einsum('oc,cyx->oyx', weights[row_tap, col_tap], window, preferred_el...  51.2 us
    ppermute x3, waiting for transfers between devices, grow_blocks(): other = lax.ppermute(tiles, axis, [(i, i ^ distance) for i in range(size)])  31.8 us
    dot_general x1, matrix products, shards(): jnp.einsum('kc,cyx->kyx', classify, second, preferred_element_type=jnp.fl...  13.2 us
    ppermute x2, starting transfers between devices, with_halo(): lax.ppermute(lax.slice_in_dim(block, block.shape[dim] - width, None, axis...  7.94 us
    ppermute x3, starting transfers between devices, grow_blocks(): other = lax.ppermute(tiles, axis, [(i, i ^ distance) for i in range(size)])  5.57 us
    all_to_all x1, waiting for transfers between devices, shards(): lax.all_to_all(outgoing, 'member', split_axis=0, concat_axis=0, tiled=True)  5.05 us
    unnamed x17, local copies, waits for them, and re-layouts  4.7 us
    dot_general x2, matrix products, shards(): jnp.einsum('iy,cyj->icj', row_part, widened, preferred_element_type=jnp.f...  3.89 us
  transfers between devices with their start and end apart: 8, of which 5 were waited for; matrix products, arithmetic and copies ran while one was open for 4% of the time, Pallas kernels for 0%

profile of v1, /device:TPU:0, one launch (start us, length us, event | category | flops | bytes accessed | tf_op | source)
XLA Modules:
  0.0 147.8 jit_solution(1769030677341943971)
XLA Ops:
  0.0 1.3 fusion.174
  4.0 4.3 %copy.12 = bf16[1,256,16,256]{1,3,2,0:T(8,128)(2,1)} copy(bf16[1,256,16,256]{3,2,1,0:T(8,128)(2,1)} %param.8) | data formatting | bytes 4194304 | tf_op args[0]
  8.3 0.1 fusion.151
  8.3 2.1 %bitcast_multiply_fusion = bf16[256,16,256]{0,2,1:T(8,128)(2,1)S(1)} fusion(bf16[1,256,16,256]{1,3,2,0:T(8,128)(2,1)} %copy.12, bf16[16,256]{1,0:T(8,128)(2,1)S(1)} %get-tuple-element.27), kind=kLoop, calls=%fused_computation.54 | loop fusion | flops 1048576 | bytes 4202496 | tf_op jit(solution)/shard_map/mul | solution.py:108
  10.4 2.5 %collective-permute-start = (bf16[256,1,256]{0,2,1:T(8,128)(2,1)S(1)}, bf16[256,1,256]{0,2,1:T(8,128)(2,1)S(1)}, u32[]{:S(2)}, u32[]{:S(2)}) collective-permute-start(bf16[256,1,256]{0,2,1:T(8,128)(2,1)S(1)} %get-tuple-element.15), channel_id=1, source_target_pairs={{0,2},{2,4},{4,6},{6,8},{8,10},{10,12},{12,14},{1,3},{3,5},{5,7},{... | collective-permute-start | bytes 393224 | tf_op jit(solution)/shard_map/ppermute | solution.py:35
  12.9 1.3 collective-permute-start.1
  14.3 0.1 multiply_bitcast_fusion
  14.4 1.7 %fusion.52 = f32[16,256,256]{2,1,0:T(8,128)S(1)} fusion(bf16[256,16,256]{2,1,0:T(8,128)(2,1)S(1)} %multiply_bitcast_fusion, bf16[3,3,256,256]{3,2,1,0:T(8,128)(2,1)S(1)} %copy-done.2), kind=kOutput, calls=%fused_computation.55 | convolution fusion | flops 536870912 | bytes 6422528 | tf_op jit(solution)/shard_map/oc,cyx->oyx/dot_general | solution.py:69
  16.1 2.3 %collective-permute-done.1 = bf16[256,1,256]{0,2,1:T(8,128)(2,1)S(1)} collective-permute-done((bf16[256,1,256]{0,2,1:T(8,128)(2,1)S(1)}, bf16[256,1,256]{0,2,1:T(8,128)(2,1)S(1)}, u32[]{:S(2)}, u32[]{:S(2)}) %collective-permute-start.1) | collective-permute-done | bytes 131104 | tf_op jit(solution)/shard_map/ppermute | solution.py:38
  18.4 0.8 fusion.5
  19.2 0.7 fusion.40
  20.0 2.8 %fusion.42 = f32[16,256,256]{2,1,0:T(8,128)} fusion(bf16[256,18,258]{0,2,1:T(8,128)(2,1)S(1)} %fusion.5, bf16[3,3,256,256]{3,2,1,0:T(8,128)(2,1)S(1)} %copy-done.2), kind=kOutput, calls=%fused_computation.44 | convolution fusion | flops 536870912 | bytes 6422528 | tf_op jit(solution)/shard_map/oc,cyx->oyx/dot_general | solution.py:69
  22.7 2.7 %fusion.44 = f32[16,256,256]{2,1,0:T(8,128)} fusion(bf16[256,18,258]{0,2,1:T(8,128)(2,1)S(1)} %fusion.5, bf16[3,3,256,256]{3,2,1,0:T(8,128)(2,1)S(1)} %copy-done.2), kind=kOutput, calls=%fused_computation.46 | convolution fusion | flops 536870912 | bytes 6422528 | tf_op jit(solution)/shard_map/oc,cyx->oyx/dot_general | solution.py:69
  25.5 2.7 %fusion.46 = f32[16,256,256]{2,1,0:T(8,128)} fusion(bf16[256,18,258]{0,2,1:T(8,128)(2,1)S(1)} %fusion.5, bf16[3,3,256,256]{3,2,1,0:T(8,128)(2,1)S(1)} %copy-done.2), kind=kOutput, calls=%fused_computation.48 | convolution fusion | flops 536870912 | bytes 6422528 | tf_op jit(solution)/shard_map/oc,cyx->oyx/dot_general | solution.py:69
  28.2 2.7 %fusion.48 = f32[16,256,256]{2,1,0:T(8,128)} fusion(bf16[256,18,258]{0,2,1:T(8,128)(2,1)S(1)} %fusion.5, bf16[3,3,256,256]{3,2,1,0:T(8,128)(2,1)S(1)} %copy-done.2), kind=kOutput, calls=%fused_computation.50 | convolution fusion | flops 536870912 | bytes 6422528 | tf_op jit(solution)/shard_map/oc,cyx->oyx/dot_general | solution.py:69
  30.9 2.8 %fusion.6 = f32[16,256,256]{2,1,0:T(8,128)} fusion(bf16[256,16,256]{0,2,1:T(8,128)(2,1)S(1)} %bitcast_multiply_fusion, bf16[256,1,256]{0,2,1:T(8,128)(2,1)S(1)} %collective-permute-done, bf16[3,3,256,256]{3,2,1,0:T(8,128)(2,1)S(1)} %copy-done.2), kind=kOutput, calls=%fused_computation.12 | convolution fusion | flops 541327360 | bytes 6553600 | tf_op jit(solution)/shard_map/oc,cyx->oyx/dot_general | solution.py:69
  33.6 2.7 %fusion.10 = f32[16,256,256]{2,1,0:T(8,128)} fusion(bf16[256,1,256]{0,2,1:T(8,128)(2,1)S(1)} %collective-permute-done.1, bf16[256,16,256]{0,2,1:T(8,128)(2,1)S(1)} %bitcast_multiply_fusion, bf16[3,3,256,256]{3,2,1,0:T(8,128)(2,1)S(1)} %copy-done.2), kind=kOutput, calls=%fused_computation.16 | convolution fusion | flops 541327360 | bytes 6553600 | tf_op jit(solution)/shard_map/oc,cyx->oyx/dot_general | solution.py:69
  36.3 9.7 %fusion.54 = bf16[256,16,256]{0,2,1:T(8,128)(2,1)S(1)} fusion(f32[16,256]{1,0:T(8,128)S(1)} %get-tuple-element.28, f32[256]{0:T(256)S(1)} %copy-done.5, bf16[256,18,258]{0,2,1:T(8,128)(2,1)S(1)} %fusion.5, f32[16,256,256]{2,1,0:T(8,128)} %fusion.10, f32[16,256,256]{2,1,0:T(8,128)S(1)} %fusion.40, f32[16,256,256]{2,1,0:T(8,128)} %fusion.42, ...), kind=kOutput, calls=%fused_computation.59 | convolution fusion | flops 549453824 | bytes 37897216 | tf_op jit(solution)/shard_map/oc,cyx->oyx/dot_general | solution.py:69
  46.1 5.4 %collective-permute-start.2 = (bf16[256,1,256]{0,2,1:T(8,128)(2,1)S(1)}, bf16[256,1,256]{0,2,1:T(8,128)(2,1)S(1)}, u32[]{:S(2)}, u32[]{:S(2)}) collective-permute-start(bf16[256,1,256]{0,2,1:T(8,128)(2,1)S(1)} %get-tuple-element.13), channel_id=1, source_target_pairs={{0,2},{2,4},{4,6},{6,8},{8,10},{10,12},{12,14},{1,3},{3,5},{5,7},{... | collective-permute-start | bytes 393224 | tf_op jit(solution)/shard_map/ppermute | solution.py:35
  51.5 1.5 collective-permute-start.3
  53.0 3.6 %fusion.112 = f32[16,256,256]{2,1,0:T(8,128)} fusion(bf16[256,16,256]{0,2,1:T(8,128)(2,1)S(1)} %fusion.54, bf16[3,3,256,256]{3,2,1,0:T(8,128)(2,1)} %param.12), kind=kOutput, calls=%fused_computation.100 | convolution fusion | flops 536870912 | bytes 6422528 | tf_op jit(solution)/shard_map/oc,cyx->oyx/dot_general | solution.py:69
  56.6 0.9 select_maximum_fusion
  57.5 0.4 copy-done.3
  57.9 2.8 %fusion.26 = f32[16,256,256]{2,1,0:T(8,128)} fusion(bf16[256,18,258]{0,2,1:T(8,128)(2,1)S(1)} %select_maximum_fusion, bf16[3,3,256,256]{3,2,1,0:T(8,128)(2,1)S(1)} %copy-done.3), kind=kOutput, calls=%fused_computation.30 | convolution fusion | flops 536870912 | bytes 6422528 | tf_op jit(solution)/shard_map/oc,cyx->oyx/dot_general | solution.py:69
  60.7 2.7 %fusion.28 = f32[16,256,256]{2,1,0:T(8,128)} fusion(bf16[256,18,258]{0,2,1:T(8,128)(2,1)S(1)} %select_maximum_fusion, bf16[3,3,256,256]{3,2,1,0:T(8,128)(2,1)S(1)} %copy-done.3), kind=kOutput, calls=%fused_computation.32 | convolution fusion | flops 536870912 | bytes 6422528 | tf_op jit(solution)/shard_map/oc,cyx->oyx/dot_general | solution.py:69
  63.4 2.7 %fusion.30 = f32[16,256,256]{2,1,0:T(8,128)} fusion(bf16[256,18,258]{0,2,1:T(8,128)(2,1)S(1)} %select_maximum_fusion, bf16[3,3,256,256]{3,2,1,0:T(8,128)(2,1)S(1)} %copy-done.3), kind=kOutput, calls=%fused_computation.34 | convolution fusion | flops 536870912 | bytes 6422528 | tf_op jit(solution)/shard_map/oc,cyx->oyx/dot_general | solution.py:69
  66.1 2.8 %fusion.32 = f32[16,256,256]{2,1,0:T(8,128)} fusion(bf16[256,18,258]{0,2,1:T(8,128)(2,1)S(1)} %select_maximum_fusion, bf16[3,3,256,256]{3,2,1,0:T(8,128)(2,1)S(1)} %copy-done.3), kind=kOutput, calls=%fused_computation.36 | convolution fusion | flops 536870912 | bytes 6422528 | tf_op jit(solution)/shard_map/oc,cyx->oyx/dot_general | solution.py:69
  68.9 2.7 %fusion.34 = f32[16,256,256]{2,1,0:T(8,128)} fusion(bf16[256,18,258]{0,2,1:T(8,128)(2,1)S(1)} %select_maximum_fusion, bf16[3,3,256,256]{3,2,1,0:T(8,128)(2,1)S(1)} %copy-done.3), kind=kOutput, calls=%fused_computation.38 | convolution fusion | flops 536870912 | bytes 6422528 | tf_op jit(solution)/shard_map/oc,cyx->oyx/dot_general | solution.py:69
  71.6 2.7 %fusion.14 = f32[16,256,256]{2,1,0:T(8,128)} fusion(bf16[256,16,256]{0,2,1:T(8,128)(2,1)S(1)} %fusion.54, bf16[256,1,256]{0,2,1:T(8,128)(2,1)S(1)} %collective-permute-done.2, bf16[3,3,256,256]{3,2,1,0:T(8,128)(2,1)S(1)} %copy-done.3), kind=kOutput, calls=%fused_computation.20 | convolution fusion | flops 541327360 | bytes 6553600 | tf_op jit(solution)/shard_map/oc,cyx->oyx/dot_general | solution.py:69
  74.4 2.7 %fusion.18 = f32[16,256,256]{2,1,0:T(8,128)} fusion(bf16[256,1,256]{0,2,1:T(8,128)(2,1)S(1)} %collective-permute-done.3, bf16[256,16,256]{0,2,1:T(8,128)(2,1)S(1)} %fusion.54, bf16[3,3,256,256]{3,2,1,0:T(8,128)(2,1)S(1)} %copy-done.3), kind=kOutput, calls=%fused_computation.24 | convolution fusion | flops 541327360 | bytes 6553600 | tf_op jit(solution)/shard_map/oc,cyx->oyx/dot_general | solution.py:69
  77.1 13.2 %fusion.72 = bf16[1,19,16,256]{3,1,2,0:T(8,128)(2,1)S(1)} fusion(f32[16,256]{1,0:T(8,128)S(1)} %get-tuple-element.28, f32[256]{0:T(256)S(1)} %copy-done.6, bf16[256,18,258]{0,2,1:T(8,128)(2,1)S(1)} %select_maximum_fusion, f32[16,256,256]{2,1,0:T(8,128)} %fusion.18, f32[16,256,256]{2,1,0:T(8,128)} %fusion.26, f32[16,256,256]{2,1,0:T(8,128)} %fusion.28, ...), kind=kOutput, calls=%fused_computation.66 | convolution fusion | flops 589455360 | bytes 35968512 | tf_op jit(solution)/shard_map/kc,cyx->kyx/dot_general | solution.py:116
  90.2 1.2 collective-permute-start.4
  91.4 1.1 collective-permute-done.4
  92.6 1.7 %collective-permute-start.5 = (bf16[2,19,16,256]{3,1,2,0:T(8,128)(2,1)S(1)}, bf16[2,19,16,256]{3,1,2,0:T(8,128)(2,1)S(1)}, u32[]{:S(2)}, u32[]{:S(2)}) collective-permute-start(bf16[2,19,16,256]{3,1,2,0:T(8,128)(2,1)S(1)} %pad_maximum_fusion.2), channel_id=1, source_target_pairs={{0,4},{2,6},{4,0},{6,2},{8,12},{10,14},{12,8},{14,10},{1,5},{3,7},... | collective-permute-start | bytes 933896 | tf_op jit(solution)/shard_map/ppermute | solution.py:19
  94.2 9.8 %collective-permute-done.5 = bf16[2,19,16,256]{3,1,2,0:T(8,128)(2,1)S(1)} collective-permute-done((bf16[2,19,16,256]{3,1,2,0:T(8,128)(2,1)S(1)}, bf16[2,19,16,256]{3,1,2,0:T(8,128)(2,1)S(1)}, u32[]{:S(2)}, u32[]{:S(2)}) %collective-permute-start.5) | collective-permute-done | bytes 311328 | tf_op jit(solution)/shard_map/ppermute | solution.py:19
  104.0 0.1 broadcast_select_fusion.3
  104.1 0.1 pad_maximum_fusion.1
  104.2 0.1 copy.15
  104.3 2.7 %collective-permute-start.6 = (bf16[4,19,16,256]{3,2,1,0:T(8,128)(2,1)S(1)}, bf16[4,19,16,256]{3,2,1,0:T(8,128)(2,1)S(1)}, u32[]{:S(2)}, u32[]{:S(2)}) collective-permute-start(bf16[4,19,16,256]{3,2,1,0:T(8,128)(2,1)S(1)} %copy.15), channel_id=1, source_target_pairs={{0,8},{2,10},{4,12},{6,14},{8,0},{10,2},{12,4},{14,6},{1,9},{3,11}... | collective-permute-start | bytes 1867784 | tf_op jit(solution)/shard_map/ppermute | solution.py:19
  107.0 0.6 fusion.186
  113.1 21.0 %collective-permute-done.6 = bf16[4,19,16,256]{3,2,1,0:T(8,128)(2,1)S(1)} collective-permute-done((bf16[4,19,16,256]{3,2,1,0:T(8,128)(2,1)S(1)}, bf16[4,19,16,256]{3,2,1,0:T(8,128)(2,1)S(1)}, u32[]{:S(2)}, u32[]{:S(2)}) %collective-permute-start.6) | collective-permute-done | bytes 622624 | tf_op jit(solution)/shard_map/ppermute | solution.py:19
  134.1 0.3 broadcast_select_fusion.1
  134.4 0.2 pad_maximum_fusion
  134.6 0.7 pad_maximum_fusion.3
  135.3 3.4 %all-to-all-start = ((bf16[2,19,10,256]{3,1,2,0:T(8,128)(2,1)}), bf16[2,19,10,256]{3,1,2,0:T(8,128)(2,1)S(1)}, u32[]{:S(2)}, u32[]{:S(2)}) async-start(bf16[2,19,10,256]{3,1,2,0:T(8,128)(2,1)} %pad_maximum_fusion.3), calls=%async_computation | async-start | bytes 491520 | tf_op jit(solution)/shard_map/all_to_all | solution.py:131
  138.8 5.0 %all-to-all-done = bf16[2,19,10,256]{3,1,2,0:T(8,128)(2,1)S(1)} async-done(((bf16[2,19,10,256]{3,1,2,0:T(8,128)(2,1)}), bf16[2,19,10,256]{3,1,2,0:T(8,128)(2,1)S(1)}, u32[]{:S(2)}, u32[]{:S(2)}) %all-to-all-start) | async-done | bytes 194592 | tf_op jit(solution)/shard_map/all_to_all | solution.py:131
  143.9 1.2 fusion.61
  145.1 2.7 %convolution_add_fusion = f32[32,19,1024]{2,0,1:T(8,128)} fusion(f32[32,19,1024]{2,0,1:T(8,128)S(1)} %fusion.61, f32[1024]{0:T(1024)S(1)} %get-tuple-element.39, s32[1024]{0:T(1024)S(1)} %get-tuple-element.42, f32[1024]{0:T(1024)S(1)} %get-tuple-element.40, s32[1024]{0:T(1024)S(1)} %get-tuple-element.41, bf16[19,10,256]{2,0,1:T(8,128)(2,1)S(1)} %get-tuple-element.25, ...), kind=kOutput, calls=%fused_computation.58 | convolution fusion | flops 114458816 | bytes 5094916 | tf_op jit(solution)/shard_map/iy,cyj->icj/dot_general | solution.py:146
  (32 shorter events, 0.4 us)
Async XLA Ops:
  0.0 77.1 %copy-start = (bf16[19,256]{1,0:T(8,128)(2,1)S(1)}, bf16[19,256]{1,0:T(8,128)(2,1)}, u32[]{:S(2)}) copy-start(bf16[19,256]{1,0:T(8,128)(2,1)} %param.14) | copy-start | bytes 29188
  8.2 6.0 %copy-start.1 = (bf16[1,256,16,256]{3,2,1,0:T(8,128)(2,1)S(1)}, bf16[1,256,16,256]{3,2,1,0:T(8,128)(2,1)}, u32[]{:S(2)}) copy-start(bf16[1,256,16,256]{3,2,1,0:T(8,128)(2,1)} %param.8) | copy-start | bytes 6291460
  10.4 4.0 %copy-start.2 = (bf16[3,3,256,256]{3,2,1,0:T(8,128)(2,1)S(1)}, bf16[3,3,256,256]{3,2,1,0:T(8,128)(2,1)}, u32[]{:S(2)}) copy-start(bf16[3,3,256,256]{3,2,1,0:T(8,128)(2,1)} %param.10) | copy-start | bytes 3538948
  10.4 5.6 %collective-permute-start = (bf16[256,1,256]{0,2,1:T(8,128)(2,1)S(1)}, bf16[256,1,256]{0,2,1:T(8,128)(2,1)S(1)}, u32[]{:S(2)}, u32[]{:S(2)}) collective-permute-start(bf16[256,1,256]{0,2,1:T(8,128)(2,1)S(1)} %get-tuple-element.15), channel_id=1, source_target_pairs={{0,2},{2,4},{4,6},{6,8},{8,10},{10,12},{12,14},{1,3},{3,5},{5,7},{... | collective-permute-start | bytes 393224 | tf_op jit(solution)/shard_map/ppermute | solution.py:35
  12.9 5.4 %collective-permute-start.1 = (bf16[256,1,256]{0,2,1:T(8,128)(2,1)S(1)}, bf16[256,1,256]{0,2,1:T(8,128)(2,1)S(1)}, u32[]{:S(2)}, u32[]{:S(2)}) collective-permute-start(bf16[256,1,256]{0,2,1:T(8,128)(2,1)S(1)} %get-tuple-element.16), channel_id=1, source_target_pairs={{2,0},{4,2},{6,4},{8,6},{10,8},{12,10},{14,12},{3,1},{5,3},{7,5},{... | collective-permute-start | bytes 393224 | tf_op jit(solution)/shard_map/ppermute | solution.py:38
  33.6 2.7 %copy-start.5 = (f32[256]{0:T(256)S(1)}, f32[256]{0:T(256)}, u32[]{:S(2)}) copy-start(f32[256]{0:T(256)} %param.11) | copy-start | bytes 3076
  46.1 10.5 %collective-permute-start.2 = (bf16[256,1,256]{0,2,1:T(8,128)(2,1)S(1)}, bf16[256,1,256]{0,2,1:T(8,128)(2,1)S(1)}, u32[]{:S(2)}, u32[]{:S(2)}) collective-permute-start(bf16[256,1,256]{0,2,1:T(8,128)(2,1)S(1)} %get-tuple-element.13), channel_id=1, source_target_pairs={{0,2},{2,4},{4,6},{6,8},{8,10},{10,12},{12,14},{1,3},{3,5},{5,7},{... | collective-permute-start | bytes 393224 | tf_op jit(solution)/shard_map/ppermute | solution.py:35
  51.5 5.1 %collective-permute-start.3 = (bf16[256,1,256]{0,2,1:T(8,128)(2,1)S(1)}, bf16[256,1,256]{0,2,1:T(8,128)(2,1)S(1)}, u32[]{:S(2)}, u32[]{:S(2)}) collective-permute-start(bf16[256,1,256]{0,2,1:T(8,128)(2,1)S(1)} %get-tuple-element.14), channel_id=1, source_target_pairs={{2,0},{4,2},{6,4},{8,6},{10,8},{12,10},{14,12},{3,1},{5,3},{7,5},{... | collective-permute-start | bytes 393224 | tf_op jit(solution)/shard_map/ppermute | solution.py:38
  56.6 1.3 copy-start.3
  74.3 2.7 %copy-start.6 = (f32[256]{0:T(256)S(1)}, f32[256]{0:T(256)}, u32[]{:S(2)}) copy-start(f32[256]{0:T(256)} %param.13) | copy-start | bytes 3076
  74.3 2.7 %copy-start.7 = (f32[19]{0:T(128)S(1)}, f32[19]{0:T(128)}, u32[]{:S(2)}) copy-start(f32[19]{0:T(128)} %param.15) | copy-start | bytes 232
  90.2 2.2 %collective-permute-start.4 = (bf16[1,19,16,256]{3,1,2,0:T(8,128)(2,1)S(1)}, bf16[1,19,16,256]{3,1,2,0:T(8,128)(2,1)S(1)}, u32[]{:S(2)}, u32[]{:S(2)}) collective-permute-start(bf16[1,19,16,256]{3,1,2,0:T(8,128)(2,1)S(1)} %fusion.72), channel_id=1, source_target_pairs={{0,2},{2,0},{4,6},{6,4},{8,10},{10,8},{12,14},{14,12},{1,3},{3,1},... | collective-permute-start | bytes 466952 | tf_op jit(solution)/shard_map/ppermute | solution.py:19
  92.5 14.5 %copy-start.4 = (s32[2]{0:T(128)S(1)}, s32[2]{0:T(128)}, u32[]{:S(2)}) copy-start(s32[2]{0:T(128)} %param.9) | copy-start | bytes 28
  92.6 11.5 %collective-permute-start.5 = (bf16[2,19,16,256]{3,1,2,0:T(8,128)(2,1)S(1)}, bf16[2,19,16,256]{3,1,2,0:T(8,128)(2,1)S(1)}, u32[]{:S(2)}, u32[]{:S(2)}) collective-permute-start(bf16[2,19,16,256]{3,1,2,0:T(8,128)(2,1)S(1)} %pad_maximum_fusion.2), channel_id=1, source_target_pairs={{0,4},{2,6},{4,0},{6,2},{8,12},{10,14},{12,8},{14,10},{1,5},{3,7},... | collective-permute-start | bytes 933896 | tf_op jit(solution)/shard_map/ppermute | solution.py:19
  104.3 29.8 %collective-permute-start.6 = (bf16[4,19,16,256]{3,2,1,0:T(8,128)(2,1)S(1)}, bf16[4,19,16,256]{3,2,1,0:T(8,128)(2,1)S(1)}, u32[]{:S(2)}, u32[]{:S(2)}) collective-permute-start(bf16[4,19,16,256]{3,2,1,0:T(8,128)(2,1)S(1)} %copy.15), channel_id=1, source_target_pairs={{0,8},{2,10},{4,12},{6,14},{8,0},{10,2},{12,4},{14,6},{1,9},{3,11}... | collective-permute-start | bytes 1867784 | tf_op jit(solution)/shard_map/ppermute | solution.py:19
  135.3 8.5 %all-to-all-start = ((bf16[2,19,10,256]{3,1,2,0:T(8,128)(2,1)}), bf16[2,19,10,256]{3,1,2,0:T(8,128)(2,1)S(1)}, u32[]{:S(2)}, u32[]{:S(2)}) async-start(bf16[2,19,10,256]{3,1,2,0:T(8,128)(2,1)} %pad_maximum_fusion.3), calls=%async_computation | async-start | bytes 491520 | tf_op jit(solution)/shard_map/all_to_all | solution.py:131
